TPU v7x, 128 devices: a whole 4x4x4 slice. The times are simulated.
128 devices in a mesh: grp: 4 (over y_lo, core), band: 32 (over y_hi, x, z).
Axes of the slice: x: 4, y: 4 (y_hi: 2, y_lo: 2; y = y_hi * 2 + y_lo), z: 4, core: 2. Of those that a mesh axis runs over, the one named last changes fastest.
Arguments:
- prior_samples: bfloat16 [32, 69, 64, 1024], P('grp', None, 'band'), may hold values from -6 to 6
- conv1_weight: bfloat16 [3, 3, 256, 69], replicated, may hold values from -0.25 to 0.25
- conv1_bias: float32 [256], replicated, may hold values from -3 to 3
- conv2_weight: bfloat16 [3, 3, 69, 256], replicated, may hold values from -0.125 to 0.125
- conv2_bias: float32 [69], replicated, may hold values from -3 to 3
- obs_index: int32 [256, 256], P(('grp', 'band')), may hold values from 0 to 17663
- obs_values: float32 [256, 256], P(('grp', 'band')), may hold values from -6 to 6
- obs_prec: float32 [256, 256], P(('grp', 'band')), may hold values from 0.25 to 4
- neighbours: int32 [256, 8], P(('grp', 'band')), may hold values from 0 to 255
- loc_weight: float32 [256, 8], P(('grp', 'band')), may hold values from 0.2 to 1
Outputs:
- analysis: float32 [32, 69, 64, 1024], P(None, None, 'band', 'grp')
Inputs may be any that keep to these rules, and one draw needn't show every extreme that they name: `neighbours`: neighbour patch numbers; a number may repeat or name the patch itself. `obs_index`: observed entry as channel * 256 + column within the patch.
All inputs are finite; a program needn't handle non-finite values.
Results may differ from a plain program's by a relative error of at most 0.0021.
Values may be sent and summed in bfloat16 or wider, within the bound.
No kernel may reach another device: no remote copies, remote signals or barrier semaphores. Data moves between devices by JAX's collectives and lax.ppermute only.
A program may use at most 128 MiB of HBM per device.

v0:
```python
import jax
import jax.numpy as jnp
import numpy as np
from jax import lax
from jax.sharding import Mesh
from jax.sharding import PartitionSpec as P

NS_ITERS = 6
GRP = ("y_lo", "core")
BAND = ("y_hi", "x", "z")
GATHER_ORDER = ("z", "x", "y_hi", "core", "y_lo")


def shift_pairs(count, step):
    return [(i, i + step) for i in range(count) if 0 <= i + step < count]


def padded_2(cells, band_size, width):
    head = lax.slice_in_dim(cells, 0, width, axis=2)
    tail = lax.slice_in_dim(cells, cells.shape[2] - width, cells.shape[2], axis=2)
    return jnp.concatenate(
        [
            lax.ppermute(tail, BAND, shift_pairs(band_size, 1)),
            cells,
            lax.ppermute(head, BAND, shift_pairs(band_size, -1)),
        ],
        axis=2,
    )


def convolve(padded, kernel, height):
    summed = jnp.zeros((kernel.shape[2], height, padded.shape[2]), jnp.float32)
    for row_shift in range(3):
        window = padded[:, row_shift : row_shift + height, :]
        for col_shift in range(3):
            shifted = jnp.roll(window, 1 - col_shift, axis=2)
            summed = summed + jnp.einsum(
                "oc,crl->orl",
                kernel[row_shift, col_shift],
                shifted,
                preferred_element_type=jnp.float32,
            )
    return summed


def make_on_device(band_size):

    def on_device(
        prior_samples,
        conv1_weight,
        conv1_bias,
        conv2_weight,
        conv2_bias,
        obs_index,
        obs_values,
        obs_prec,
        neighbours,
        loc_weight,
    ):
        highest = lax.Precision.HIGHEST
        height = prior_samples.shape[2]
        padded = padded_2(prior_samples, band_size, 1)

        def first_layer(member):
            return jax.nn.silu(
                convolve(member, conv1_weight, height) + conv1_bias[:, None, None]
            ).astype(jnp.bfloat16)

        hidden_fields = lax.map(first_layer, padded)
        northern_halo = lax.ppermute(
            hidden_fields[:, :, height - 1 :, :], BAND, shift_pairs(band_size, 1)
        )
        southern_halo = lax.ppermute(hidden_fields[:, :, :1, :], BAND, shift_pairs(band_size, -1))

        def output_layer(inputs):
            member, own_rows, above_row, below_row = inputs
            extended = jnp.concatenate([above_row, own_rows, below_row], axis=1)
            summed = (
                member.astype(jnp.float32)
                + convolve(extended, conv2_weight, height)
                + conv2_bias[:, None, None]
            )
            return summed.astype(jnp.bfloat16)

        predicted_samples = lax.map(
            output_layer, (prior_samples, hidden_fields, northern_halo, southern_halo)
        )
        patch_block_slice = lax.all_to_all(
            predicted_samples, GRP, split_axis=3, concat_axis=0, tiled=True
        )
        ensemble = patch_block_slice.shape[0]
        channels = patch_block_slice.shape[1]
        patch_width = patch_block_slice.shape[3]
        column = obs_index % patch_width
        channel = obs_index // patch_width
        column_hot = (
            column[:, :, None] == jnp.arange(patch_width, dtype=jnp.int32)[None, None, :]
        ).astype(jnp.bfloat16)
        by_column = jnp.einsum(
            "mcil,iol->icmo", patch_block_slice, column_hot, preferred_element_type=jnp.float32
        )
        channel_hot = (
            channel[:, None, :] == jnp.arange(channels, dtype=jnp.int32)[None, :, None]
        ).astype(jnp.float32)
        predicted = jnp.sum(by_column * channel_hot[:, :, None, :], axis=1)
        predicted_mean = jnp.mean(predicted, axis=1)
        perturb = predicted - predicted_mean[:, None, :]
        innovation = obs_values - predicted_mean
        gram_local = jnp.einsum("pmo,po,pno->pmn", perturb, obs_prec, perturb, precision=highest)
        pull_vec = jnp.einsum("pmo,po->pm", perturb, obs_prec * innovation, precision=highest)
        count = gram_local.shape[0]
        packed = jnp.concatenate([gram_local.reshape(count, ensemble * ensemble), pull_vec], axis=1)
        for axis in GATHER_ORDER:
            packed = lax.all_gather(packed, axis, axis=0, tiled=False)
        packed = packed.reshape(-1, ensemble * ensemble + ensemble)
        total_patches = packed.shape[0]
        patch_ids = jnp.arange(total_patches, dtype=jnp.int32)
        matches = (neighbours[:, :, None] == patch_ids[None, None, :]).astype(jnp.float32)
        spread_weights = jnp.sum(loc_weight[:, :, None] * matches, axis=1)
        summed = jnp.einsum("pj,jf->pf", spread_weights, packed, precision=highest)
        gram_sum = summed[:, : ensemble * ensemble].reshape(count, ensemble, ensemble)
        pull_sum = summed[:, ensemble * ensemble :]
        identity = jnp.broadcast_to(
            jnp.eye(ensemble, dtype=jnp.float32), (height, ensemble, ensemble)
        )
        matrix = (ensemble - 1.0) * identity + gram_local + gram_sum
        pulled = pull_vec + pull_sum
        norm_scale = jnp.sqrt(jnp.sum(matrix * matrix, axis=(1, 2)))
        sqrt_iter = matrix / norm_scale[:, None, None]
        inverse_root = identity
        for sweep in range(NS_ITERS):
            half_step = 1.5 * identity - 0.5 * jnp.einsum(
                "pab,pbc->pac", inverse_root, sqrt_iter, precision=highest
            )
            sqrt_iter = jnp.einsum("pab,pbc->pac", sqrt_iter, half_step, precision=highest)
            inverse_root = jnp.einsum("pab,pbc->pac", half_step, inverse_root, precision=highest)
        once_applied = jnp.einsum("pab,pb->pa", inverse_root, pulled, precision=highest)
        mean_weight = (
            jnp.einsum("pab,pb->pa", inverse_root, once_applied, precision=highest)
            / norm_scale[:, None]
        )
        transform = (jnp.sqrt(ensemble - 1.0) / jnp.sqrt(norm_scale))[
            :, None, None
        ] * inverse_root + mean_weight[:, :, None]
        realization_grid = jnp.transpose(patch_block_slice, (2, 0, 1, 3)).reshape(
            height, ensemble, channels * patch_width
        )
        field = realization_grid.astype(jnp.float32)
        centre = jnp.mean(field, axis=1)
        spread = field - centre[:, None, :]
        analysed = centre[:, None, :] + jnp.einsum(
            "pkm,pkc->pmc", transform, spread, precision=highest
        )
        return analysed.reshape(height, ensemble, channels, patch_width).transpose(1, 2, 0, 3)

    return on_device


def solution(mesh):
    grp_size, band_size = mesh.devices.shape
    fine = Mesh(mesh.devices.reshape(grp_size // 2, 2, 2, band_size // 32 * 4, 4), GRP + BAND)
    placed = (
        P(GRP, None, BAND, None),
        P(),
        P(),
        P(),
        P(),
        P(GRP + BAND, None),
        P(GRP + BAND, None),
        P(GRP + BAND, None),
        P(GRP + BAND, None),
        P(GRP + BAND, None),
    )
    return jax.shard_map(
        make_on_device(band_size),
        mesh=fine,
        in_specs=placed,
        out_specs=P(None, None, BAND, GRP),
        check_vma=False,
    )
```

profile of v0, /device:TPU:1, one launch (start us, length us, event | category | flops | bytes accessed | tf_op | source)
XLA Modules:
  0.0 478.3 jit_solution(13882782711208538704)
XLA Ops:
  6.5 5.9 %fusion.154 = (bf16[8,69,1,1024]{3,2,1,0:T(2,128)(2,1)S(1)}, bf16[8,69,1,1024]{3,2,1,0:T(2,128)(2,1)S(1)}) fusion(bf16[8,69,2,1024]{3,2,1,0:T(2,128)(2,1)} %param.14), kind=kLoop, calls=%fused_computation.215 | loop fusion | bytes 4521984 | tf_op jit(solution)/shard_map/slice | solution.py:20
  12.9 5.5 %collective-permute-start = (bf16[8,69,1,1024]{3,0,2,1:T(8,128)(2,1)S(1)}, bf16[8,69,1,1024]{3,0,2,1:T(8,128)(2,1)}, u32[]{:S(2)}, u32[]{:S(2)}) collective-permute-start(bf16[8,69,1,1024]{3,0,2,1:T(8,128)(2,1)S(1)} %copy.75), channel_id=1, source_target_pairs={{0,1},{1,2},{2,3},{3,4},{4,5},{5,6},{6,7},{7,8},{8,9},{9,10},{10,1... | collective-permute-start | bytes 3391496 | tf_op jit(solution)/shard_map/ppermute | solution.py:23
  18.4 1.4 copy.76
  19.8 1.3 collective-permute-start.1
  21.9 19.1 %collective-permute-done = bf16[8,69,1,1024]{3,0,2,1:T(8,128)(2,1)} collective-permute-done((bf16[8,69,1,1024]{3,0,2,1:T(8,128)(2,1)S(1)}, bf16[8,69,1,1024]{3,0,2,1:T(8,128)(2,1)}, u32[]{:S(2)}, u32[]{:S(2)}) %collective-permute-start) | collective-permute-done | bytes 1130528 | tf_op jit(solution)/shard_map/ppermute | solution.py:23
  41.0 1.9 copy.50
  42.8 4.7 collective-permute-done.1
  47.5 1.9 copy.52
  49.4 2.5 pad_maximum_fusion.6
  51.9 73.3 %while.20 = (s32[]{:T(128)}, bf16[8,256,2,1024]{3,1,2,0:T(8,128)(2,1)}, bf16[8,69,4,1024]{3,1,2,0:T(8,128)(2,1)}, bf16[3,3,256,69]{2,3,1,0:T(8,128)(2,1)S(1)}, f32[256]{0:T(256)S(1)}, /*index=5*/s32[]{:T(128)}) while((s32[]{:T(128)}, bf16[8,256,2,1024]{3,1,2,0:T(8,128)(2,1)}, bf16[8,69,4,1024]{3,1,2,0:T(8,128)(2,1)}, ...), condition=%wide.region_1.2_spmd, body=%wide.region_0.1_spmd.sunk | while | flops 661897216 | bytes 47412808 | solution.py:69
  125.2 6.1 %fusion.153 = (bf16[8,256,1,1024]{3,1,2,0:T(8,128)(2,1)}, bf16[8,256,1,1024]{3,1,2,0:T(8,128)(2,1)}) fusion(bf16[8,256,2,1024]{3,1,2,0:T(8,128)(2,1)} %get-tuple-element.324), kind=kLoop, calls=%fused_computation.214 | loop fusion | bytes 16777216 | tf_op jit(solution)/shard_map/slice | solution.py:73
  131.3 4.5 collective-permute-start.2
  135.8 1.5 collective-permute-start.3
  137.2 84.9 %collective-permute-done.2 = bf16[8,256,1,1024]{3,1,2,0:T(8,128)(2,1)} collective-permute-done((bf16[8,256,1,1024]{3,1,2,0:T(8,128)(2,1)}, bf16[8,256,1,1024]{3,1,2,0:T(8,128)(2,1)}, u32[]{:S(2)}, u32[]{:S(2)}) %collective-permute-start.2) | collective-permute-done | bytes 4194336 | tf_op jit(solution)/shard_map/ppermute | solution.py:70
  222.1 5.8 %collective-permute-done.3 = bf16[8,256,1,1024]{3,1,2,0:T(8,128)(2,1)} collective-permute-done((bf16[8,256,1,1024]{3,1,2,0:T(8,128)(2,1)}, bf16[8,256,1,1024]{3,1,2,0:T(8,128)(2,1)}, u32[]{:S(2)}, u32[]{:S(2)}) %collective-permute-start.3) | collective-permute-done | bytes 4194336 | tf_op jit(solution)/shard_map/ppermute | solution.py:73
  227.9 70.6 %while.21 = (s32[]{:T(128)}, bf16[8,69,2,1024]{3,1,2,0:T(8,128)(2,1)S(1)}, bf16[8,69,2,1024]{3,1,2,0:T(8,128)(2,1)}, bf16[8,256,1,1024]{3,1,2,0:T(8,128)(2,1)}, ...) while((s32[]{:T(128)}, ...), condition=%wide.region_3.4_spmd, body=%wide.region_2.3_spmd.sunk | while | flops 675929088 | bytes 41343592 | solution.py:85
  227.9 1.3 dynamic-slice_bitcast_fusion.9
  229.2 1.3 dynamic-slice_bitcast_fusion.8
  230.5 1.4 fusion.305
  235.4 1.3 fusion.308
  236.7 1.3 dynamic-slice_bitcast_fusion.9
  238.0 1.3 dynamic-slice_bitcast_fusion.8
  239.3 1.4 fusion.305
  244.2 1.3 fusion.308
  245.5 1.3 dynamic-slice_bitcast_fusion.9
  246.8 1.3 dynamic-slice_bitcast_fusion.8
  248.1 1.4 fusion.305
  253.1 1.3 fusion.308
  254.4 1.3 dynamic-slice_bitcast_fusion.9
  255.7 1.3 dynamic-slice_bitcast_fusion.8
  256.9 1.4 fusion.305
  261.9 1.3 fusion.308
  263.2 1.3 dynamic-slice_bitcast_fusion.9
  264.5 1.3 dynamic-slice_bitcast_fusion.8
  265.8 1.4 fusion.305
  270.7 1.3 fusion.308
  272.0 1.3 dynamic-slice_bitcast_fusion.9
  273.3 1.3 dynamic-slice_bitcast_fusion.8
  274.6 1.4 fusion.305
  279.5 1.3 fusion.308
  280.8 1.3 dynamic-slice_bitcast_fusion.9
  282.1 1.3 dynamic-slice_bitcast_fusion.8
  283.4 1.4 fusion.305
  288.4 1.3 fusion.308
  289.7 1.3 dynamic-slice_bitcast_fusion.9
  291.0 1.3 dynamic-slice_bitcast_fusion.8
  292.2 1.4 fusion.305
  297.2 1.3 fusion.308
  298.5 7.7 %copy.57 = bf16[8,69,2,1024]{1,2,0,3:T(2,128)(2,1)} copy(bf16[8,69,2,1024]{3,1,2,0:T(8,128)(2,1)S(1)} %get-tuple-element.75) | data formatting | bytes 4521984 | tf_op jit(solution)/shard_map/while | solution.py:85
  306.1 8.0 %all-to-all-start = ((bf16[8,69,2,1024]{1,2,0,3:T(2,128)(2,1)}), bf16[8,69,2,1024]{1,2,0,3:T(2,128)(2,1)}, u32[]{:S(2)}, u32[]{:S(2)}) async-start(bf16[8,69,2,1024]{1,2,0,3:T(2,128)(2,1)} %copy.57), calls=%async_computation | async-start | bytes 8388608 | tf_op jit(solution)/shard_map/all_to_all | solution.py:88
  314.2 47.3 %all-to-all-done = bf16[8,69,2,1024]{1,2,0,3:T(2,128)(2,1)} async-done(((bf16[8,69,2,1024]{1,2,0,3:T(2,128)(2,1)}), bf16[8,69,2,1024]{1,2,0,3:T(2,128)(2,1)}, u32[]{:S(2)}, u32[]{:S(2)}) %all-to-all-start) | async-done | bytes 2261024 | tf_op jit(solution)/shard_map/all_to_all | solution.py:88
  361.5 11.4 %copy.72 = bf16[8,69,2,4,256]{4,3,0,2,1:T(4,128)(2,1)} copy(bf16[8,69,2,4,256]{1,2,0,4,3:T(2,128)(2,1)} %bitcast.45) | data formatting | bytes 4521984 | tf_op jit(solution)/shard_map/all_to_all | solution.py:88
  372.9 2.9 copy.59
  377.3 9.3 %all-gather.5 = f32[4,2,1056]{2,1,0:T(2,128)S(1)} all-gather(f32[1,2,1056]{2,1,0:T(2,128)S(1)} %maximum_bitcast_fusion), channel_id=2, replica_groups=mesh['y_lo'=2,'core'=2,'y_hi'=2,'x'=4,'z'=4] {'z'}, dimensions={0}, use_global_device_ids=true | all-gather | bytes 42240 | tf_op jit(solution)/shard_map/all_gather | solution.py:114
  386.6 17.7 %all-gather.1 = f32[16,2,1056]{2,1,0:T(2,128)S(1)} all-gather(f32[4,2,1056]{2,1,0:T(2,128)S(1)} %all-gather.5), channel_id=3, replica_groups=mesh['y_lo'=2,'core'=2,'y_hi'=2,'x'=4,'z'=4] {'x'}, dimensions={0}, use_global_device_ids=true | all-gather | bytes 168960 | tf_op jit(solution)/shard_map/all_gather | solution.py:114
  404.3 6.2 %all-gather.2 = f32[8,4,2,1056]{3,1,2,0:T(4,128)S(1)} all-gather(f32[4,4,2,1056]{3,1,2,0:T(4,128)S(1)} %copy.60), channel_id=4, replica_groups=mesh['y_lo'=2,'core'=2,'y_hi'=2,'x'=4,'z'=4] {'y_hi'}, dimensions={0}, use_global_device_ids=true | all-gather | bytes 405504 | tf_op jit(solution)/shard_map/all_gather | solution.py:114
  410.5 9.4 %all-gather.3 = f32[4,4,4,2,1056]{4,2,3,1,0:T(4,128)} all-gather(f32[2,4,4,2,1056]{4,2,3,1,0:T(4,128)S(1)} %bitcast.284), channel_id=5, replica_groups=mesh['y_lo'=2,'core'=2,'y_hi'=2,'x'=4,'z'=4] {'core'}, dimensions={0}, use_global_device_ids=true | all-gather | bytes 811008 | tf_op jit(solution)/shard_map/all_gather | solution.py:114
  420.0 2.5 convert_bitcast_fusion
  422.5 5.1 %reshape.55 = f32[2,32,17664]{2,1,0:T(8,128)} reshape(f32[2,32,69,256]{3,2,1,0:T(8,128)} %convert_bitcast_fusion) | data formatting | bytes 9043968 | tf_op jit(solution)/shard_map/convert_element_type | solution.py:148
  428.1 15.9 %all-gather.8.cloned.1.call-done = f32[4,2,4,4,2,1056]{5,3,4,2,1,0:T(4,128)} async-done(((f32[2,2,4,4,2,1056]{5,3,4,2,1,0:T(4,128)}), f32[4,2,4,4,2,1056]{5,3,4,2,1,0:T(4,128)}) %all-gather.8.cloned.1.call-update) | async-done | bytes 1081360 | tf_op jit(solution)/shard_map/all_gather | solution.py:114
  444.0 1.9 copy.61
  451.0 7.4 %convolution_add_fusion.7 = f32[2,32,17664]{2,1,0:T(8,128)} fusion(f32[2,32,17664]{2,1,0:T(8,128)} %reshape.55, f32[2,17664]{1,0:T(2,128)S(1)} %bitcast.286, f32[2,32,32]{2,1,0:T(8,128)S(1)} %fusion.164, f32[2,32]{1,0:T(2,128)S(1)} %broadcast_divide_fusion.3, f32[2]{0:T(128)S(1)} %get-tuple-element.172), kind=kOutput, calls=%fused_computation.144 | convolution fusion | flops 436375552 | bytes 9193736 | tf_op jit(solution)/shard_map/pkm,pkc->pmc/dot_general | solution.py:151
  458.4 5.1 %reshape.53 = f32[2,32,69,256]{3,2,1,0:T(8,128)} reshape(f32[2,32,17664]{2,1,0:T(8,128)} %convolution_add_fusion.7) | data formatting | bytes 9043968 | tf_op jit(solution)/shard_map/reshape | solution.py:154
  463.5 7.9 %copy.63 = f32[32,69,2,256]{3,2,1,0:T(2,128)} copy(f32[32,69,2,256]{3,1,0,2:T(8,128)} %bitcast.281) | data formatting | bytes 9043968 | tf_op jit(solution)/shard_map/transpose | solution.py:154
  (255 shorter events, 109.2 us)
Async XLA Ops:
  12.9 8.3 %copy-start = (bf16[8,69,2,1024]{3,2,1,0:T(2,128)(2,1)S(1)}, bf16[8,69,2,1024]{3,2,1,0:T(2,128)(2,1)}, u32[]{:S(2)}) copy-start(bf16[8,69,2,1024]{3,2,1,0:T(2,128)(2,1)} %param.14) | copy-start | bytes 6782980
  12.9 28.1 %collective-permute-start = (bf16[8,69,1,1024]{3,0,2,1:T(8,128)(2,1)S(1)}, bf16[8,69,1,1024]{3,0,2,1:T(8,128)(2,1)}, u32[]{:S(2)}, u32[]{:S(2)}) collective-permute-start(bf16[8,69,1,1024]{3,0,2,1:T(8,128)(2,1)S(1)} %copy.75), channel_id=1, source_target_pairs={{0,1},{1,2},{2,3},{3,4},{4,5},{5,6},{6,7},{7,8},{8,9},{9,10},{10,1... | collective-permute-start | bytes 3391496 | tf_op jit(solution)/shard_map/ppermute | solution.py:23
  19.8 27.7 %collective-permute-start.1 = (bf16[8,69,1,1024]{3,0,2,1:T(8,128)(2,1)}, bf16[8,69,1,1024]{3,0,2,1:T(8,128)(2,1)}, u32[]{:S(2)}, u32[]{:S(2)}) collective-permute-start(bf16[8,69,1,1024]{3,0,2,1:T(8,128)(2,1)} %copy.76), channel_id=1, source_target_pairs={{1,0},{2,1},{3,2},{4,3},{5,4},{6,5},{7,6},{8,7},{9,8},{10,9},{11,1... | collective-permute-start | bytes 3391496 | tf_op jit(solution)/shard_map/ppermute | solution.py:25
  21.9 27.5 %copy-start.1 = (bf16[8,69,2,1024]{3,1,2,0:T(8,128)(2,1)}, bf16[8,69,2,1024]{3,1,2,0:T(8,128)(2,1)S(1)}, u32[]{:S(2)}) copy-start(bf16[8,69,2,1024]{3,1,2,0:T(8,128)(2,1)S(1)} %copy.55) | copy-start | bytes 6782980
  49.4 2.5 copy-start.2
  49.4 2.5 copy-start.4
  125.2 102.7 %copy-start.3 = (bf16[3,3,69,256]{3,2,1,0:T(8,128)(2,1)S(1)}, bf16[3,3,69,256]{3,2,1,0:T(8,128)(2,1)}, u32[]{:S(2)}) copy-start(bf16[3,3,69,256]{3,2,1,0:T(8,128)(2,1)} %param.17) | copy-start | bytes 953860
  125.2 102.7 %copy-start.10 = (f32[69]{0:T(128)S(1)}, f32[69]{0:T(128)}, u32[]{:S(2)}) copy-start(f32[69]{0:T(128)} %param.18) | copy-start | bytes 832
  131.3 90.8 %collective-permute-start.2 = (bf16[8,256,1,1024]{3,1,2,0:T(8,128)(2,1)}, bf16[8,256,1,1024]{3,1,2,0:T(8,128)(2,1)}, u32[]{:S(2)}, u32[]{:S(2)}) collective-permute-start(bf16[8,256,1,1024]{3,1,2,0:T(8,128)(2,1)} %get-tuple-element.165), channel_id=1, source_target_pairs={{0,1},{1,2},{2,3},{3,4},{4,5},{5,6},{6,7},{7,8},{8,9},{9,10},{10,1... | collective-permute-start | bytes 12582920 | tf_op jit(solution)/shard_map/ppermute | solution.py:70
  135.8 92.1 %collective-permute-start.3 = (bf16[8,256,1,1024]{3,1,2,0:T(8,128)(2,1)}, bf16[8,256,1,1024]{3,1,2,0:T(8,128)(2,1)}, u32[]{:S(2)}, u32[]{:S(2)}) collective-permute-start(bf16[8,256,1,1024]{3,1,2,0:T(8,128)(2,1)} %get-tuple-element.164), channel_id=1, source_target_pairs={{1,0},{2,1},{3,2},{4,3},{5,4},{6,5},{7,6},{8,7},{9,8},{10,9},{11,1... | collective-permute-start | bytes 12582920 | tf_op jit(solution)/shard_map/ppermute | solution.py:73
  306.1 8.0 %copy-start.6 = (s32[2,256]{1,0:T(2,128)S(1)}, s32[2,256]{1,0:T(2,128)}, u32[]{:S(2)}) copy-start(s32[2,256]{1,0:T(2,128)} %param.19) | copy-start | bytes 6148
  306.1 55.4 %all-to-all-start = ((bf16[8,69,2,1024]{1,2,0,3:T(2,128)(2,1)}), bf16[8,69,2,1024]{1,2,0,3:T(2,128)(2,1)}, u32[]{:S(2)}, u32[]{:S(2)}) async-start(bf16[8,69,2,1024]{1,2,0,3:T(2,128)(2,1)} %copy.57), calls=%async_computation | async-start | bytes 8388608 | tf_op jit(solution)/shard_map/all_to_all | solution.py:88
  314.1 129.9 %all-gather.8.cloned.1.call-start = ((), (), s32[]{:S(2)}) async-start(), calls=%async_computation.1 | async-start | bytes 1769472 | tf_op jit(solution)/shard_map/all_gather | solution.py:114
  375.8 1.0 copy-start.5
  375.8 1.0 copy-start.7
  376.8 43.2 %copy-start.8 = (f32[2,8]{1,0:T(2,128)S(1)}, f32[2,8]{1,0:T(2,128)}, u32[]{:S(2)}) copy-start(f32[2,8]{1,0:T(2,128)} %param.23) | copy-start | bytes 196
  376.8 43.2 %copy-start.9 = (s32[2,8]{1,0:T(2,128)S(1)}, s32[2,8]{1,0:T(2,128)}, u32[]{:S(2)}) copy-start(s32[2,8]{1,0:T(2,128)} %param.22) | copy-start | bytes 196
Sparse Core Ops, SparseCore 0:
  420.0 23.9 all-gather.7
where the time goes:
time: 480 us; the launch traced here: 478 us
  waiting for transfers between devices  178 us (37%)
  local copies, waits for them, and re-layouts  108 us (22%)
  matrix products  97.1 us (20%)
  blocking collectives  42.5 us (9%)
  starting transfers between devices  20.8 us (4%)
  other arithmetic  17.9 us (4%)
  between operations  13.8 us (3%)
    ppermute x1, waiting for transfers between devices, on_device(): lax.ppermute(hidden_fields[:, :, height - 1:, :], BAND, shift_pairs(band_...  84.9 us
    dot_general x144, matrix products, convolve(): jnp.einsum('oc,crl->orl', kernel[row_shift, col_shift], shifted, preferre...  84.5 us
    all_to_all x1, waiting for transfers between devices, on_device(): lax.all_to_all(predicted_samples, GRP, split_axis=3, concat_axis=0, tiled...  47.3 us
    all_gather x4, blocking collectives, on_device(): packed = lax.all_gather(packed, axis, axis=0, tiled=False)  42.5 us
    squeeze x16, local copies, waits for them, and re-layouts, on_device(): lax.map(output_layer, (prior_samples, hidden_fields, northern_halo, south...  20.6 us
    ppermute x1, waiting for transfers between devices, padded_2(): lax.ppermute(tail, BAND, shift_pairs(band_size, 1))  19.1 us
    all_gather x1, waiting for transfers between devices, on_device(): packed = lax.all_gather(packed, axis, axis=0, tiled=False)  15.9 us
    all_to_all x2, local copies, waits for them, and re-layouts, on_device(): lax.all_to_all(predicted_samples, GRP, split_axis=3, concat_axis=0, tiled...  14.3 us
  transfers between devices with their start and end apart: 6, of which 6 were waited for; matrix products, arithmetic and copies ran while one was open for 3% of the time, Pallas kernels for 0%

commit v1 on v0

--- a/solution.py
+++ b/solution.py
@@ -85,8 +85,11 @@
         predicted_samples = lax.map(
             output_layer, (prior_samples, hidden_fields, northern_halo, southern_halo)
         )
-        patch_block_slice = lax.all_to_all(
-            predicted_samples, GRP, split_axis=3, concat_axis=0, tiled=True
+        patch_block_slice = jnp.concatenate(
+            lax.all_to_all(
+                jnp.stack(jnp.split(predicted_samples, lax.axis_size(GRP), axis=3)), GRP, 0, 0
+            ),
+            axis=0,
         )
         ensemble = patch_block_slice.shape[0]
         channels = patch_block_slice.shape[1]

time: 480 us -> 443 us (0.923)
  waiting for transfers between devices: 178 us -> 157 us
  local copies, waits for them, and re-layouts: 108 us -> 89.6 us
    all_to_all x1, waiting for transfers between devices: 47.3 us -> 26.6 us  [on_device(): lax.all_to_all(jnp.stack(jnp.split(predicted_samples, lax.axis_size(GRP),...]
    all_to_all x2 -> x1, local copies, waits for them, and re-layouts: 14.3 us -> 2.43 us  [on_device(): lax.all_to_all(jnp.stack(jnp.split(predicted_samples, lax.axis_size(GRP),...]
    while x2, local copies, waits for them, and re-layouts: 8.39 us -> 1.98 us  [on_device(): lax.map(output_layer, (prior_samples, hidden_fields, northern_halo, south...]
where the time goes in v1:
time: 443 us; the launch traced here: 441 us
  waiting for transfers between devices  157 us (35%)
  matrix products  97.1 us (22%)
  local copies, waits for them, and re-layouts  89.6 us (20%)
  blocking collectives  42.5 us (10%)
  starting transfers between devices  20.4 us (5%)
  other arithmetic  19.5 us (4%)
  between operations  13.8 us (3%)
    ppermute x1, waiting for transfers between devices, on_device(): lax.ppermute(hidden_fields[:, :, height - 1:, :], BAND, shift_pairs(band_...  84.8 us
    dot_general x144, matrix products, convolve(): jnp.einsum('oc,crl->orl', kernel[row_shift, col_shift], shifted, preferre...  84.6 us
    all_gather x4, blocking collectives, on_device(): packed = lax.all_gather(packed, axis, axis=0, tiled=False)  42.5 us
    all_to_all x1, waiting for transfers between devices, on_device(): lax.all_to_all(jnp.stack(jnp.split(predicted_samples, lax.axis_size(GRP),...  26.6 us
    squeeze x16, local copies, waits for them, and re-layouts, on_device(): lax.map(output_layer, (prior_samples, hidden_fields, northern_halo, south...  20.6 us
    ppermute x1, waiting for transfers between devices, padded_2(): lax.ppermute(tail, BAND, shift_pairs(band_size, 1))  19.1 us
    all_gather x1, waiting for transfers between devices, on_device(): packed = lax.all_gather(packed, axis, axis=0, tiled=False)  15.9 us
    dynamic_update_slice x16, local copies, waits for them, and re-layouts, on_device(): hidden_fields = lax.map(first_layer, padded)  12.8 us
  transfers between devices with their start and end apart: 6, of which 6 were waited for; matrix products, arithmetic and copies ran while one was open for 3% of the time, Pallas kernels for 0%

profile of v1, /device:TPU:1, one launch (start us, length us, event | category | flops | bytes accessed | tf_op | source)
XLA Modules:
  0.0 440.9 jit_solution(17949535680139955369)
XLA Ops:
  6.5 5.9 %fusion.154 = (bf16[8,69,1,1024]{3,2,1,0:T(2,128)(2,1)S(1)}, bf16[8,69,1,1024]{3,2,1,0:T(2,128)(2,1)S(1)}) fusion(bf16[8,69,2,1024]{3,2,1,0:T(2,128)(2,1)} %param.14), kind=kLoop, calls=%fused_computation.220 | loop fusion | bytes 4521984 | tf_op jit(solution)/shard_map/slice | solution.py:20
  12.9 5.5 %collective-permute-start = (bf16[8,69,1,1024]{3,0,2,1:T(8,128)(2,1)S(1)}, bf16[8,69,1,1024]{3,0,2,1:T(8,128)(2,1)}, u32[]{:S(2)}, u32[]{:S(2)}) collective-permute-start(bf16[8,69,1,1024]{3,0,2,1:T(8,128)(2,1)S(1)} %copy.77), channel_id=1, source_target_pairs={{0,1},{1,2},{2,3},{3,4},{4,5},{5,6},{6,7},{7,8},{8,9},{9,10},{10,1... | collective-permute-start | bytes 3391496 | tf_op jit(solution)/shard_map/ppermute | solution.py:23
  18.4 1.4 copy.78
  19.8 1.3 collective-permute-start.1
  21.9 19.1 %collective-permute-done = bf16[8,69,1,1024]{3,0,2,1:T(8,128)(2,1)} collective-permute-done((bf16[8,69,1,1024]{3,0,2,1:T(8,128)(2,1)S(1)}, bf16[8,69,1,1024]{3,0,2,1:T(8,128)(2,1)}, u32[]{:S(2)}, u32[]{:S(2)}) %collective-permute-start) | collective-permute-done | bytes 1130528 | tf_op jit(solution)/shard_map/ppermute | solution.py:23
  41.0 1.9 copy.51
  42.8 4.7 %collective-permute-done.1 = bf16[8,69,1,1024]{3,0,2,1:T(8,128)(2,1)} collective-permute-done((bf16[8,69,1,1024]{3,0,2,1:T(8,128)(2,1)}, bf16[8,69,1,1024]{3,0,2,1:T(8,128)(2,1)}, u32[]{:S(2)}, u32[]{:S(2)}) %collective-permute-start.1) | collective-permute-done | bytes 1130528 | tf_op jit(solution)/shard_map/ppermute | solution.py:25
  47.5 1.9 copy.53
  49.4 2.5 pad_maximum_fusion.6
  51.9 73.3 %while.20 = (s32[]{:T(128)}, bf16[8,256,2,1024]{3,1,2,0:T(8,128)(2,1)}, bf16[8,69,4,1024]{3,1,2,0:T(8,128)(2,1)}, bf16[3,3,256,69]{2,3,1,0:T(8,128)(2,1)S(1)}, f32[256]{0:T(256)S(1)}, /*index=5*/s32[]{:T(128)}) while((s32[]{:T(128)}, bf16[8,256,2,1024]{3,1,2,0:T(8,128)(2,1)}, bf16[8,69,4,1024]{3,1,2,0:T(8,128)(2,1)}, ...), condition=%wide.region_1.2_spmd, body=%wide.region_0.1_spmd.sunk | while | flops 661897216 | bytes 47412808 | solution.py:69
  125.3 6.1 %fusion.153 = (bf16[8,256,1,1024]{3,1,2,0:T(8,128)(2,1)}, bf16[8,256,1,1024]{3,1,2,0:T(8,128)(2,1)}) fusion(bf16[8,256,2,1024]{3,1,2,0:T(8,128)(2,1)} %get-tuple-element.328), kind=kLoop, calls=%fused_computation.219 | loop fusion | bytes 16777216 | tf_op jit(solution)/shard_map/slice | solution.py:73
  131.3 4.5 %collective-permute-start.2 = (bf16[8,256,1,1024]{3,1,2,0:T(8,128)(2,1)}, bf16[8,256,1,1024]{3,1,2,0:T(8,128)(2,1)}, u32[]{:S(2)}, u32[]{:S(2)}) collective-permute-start(bf16[8,256,1,1024]{3,1,2,0:T(8,128)(2,1)} %get-tuple-element.165), channel_id=1, source_target_pairs={{0,1},{1,2},{2,3},{3,4},{4,5},{5,6},{6,7},{7,8},{8,9},{9,10},{10,1... | collective-permute-start | bytes 12582920 | tf_op jit(solution)/shard_map/ppermute | solution.py:70
  135.8 1.5 collective-permute-start.3
  137.3 84.8 %collective-permute-done.2 = bf16[8,256,1,1024]{3,1,2,0:T(8,128)(2,1)} collective-permute-done((bf16[8,256,1,1024]{3,1,2,0:T(8,128)(2,1)}, bf16[8,256,1,1024]{3,1,2,0:T(8,128)(2,1)}, u32[]{:S(2)}, u32[]{:S(2)}) %collective-permute-start.2) | collective-permute-done | bytes 4194336 | tf_op jit(solution)/shard_map/ppermute | solution.py:70
  222.1 5.8 %collective-permute-done.3 = bf16[8,256,1,1024]{3,1,2,0:T(8,128)(2,1)} collective-permute-done((bf16[8,256,1,1024]{3,1,2,0:T(8,128)(2,1)}, bf16[8,256,1,1024]{3,1,2,0:T(8,128)(2,1)}, u32[]{:S(2)}, u32[]{:S(2)}) %collective-permute-start.3) | collective-permute-done | bytes 4194336 | tf_op jit(solution)/shard_map/ppermute | solution.py:73
  227.9 70.6 %while.21 = (s32[]{:T(128)}, bf16[8,69,2,1024]{3,1,2,0:T(8,128)(2,1)S(1)}, bf16[8,69,2,1024]{3,1,2,0:T(8,128)(2,1)}, bf16[8,256,1,1024]{3,1,2,0:T(8,128)(2,1)}, ...) while((s32[]{:T(128)}, ...), condition=%wide.region_3.4_spmd, body=%wide.region_2.3_spmd.sunk | while | flops 675929088 | bytes 41343592 | solution.py:85
  227.9 1.3 dynamic-slice_bitcast_fusion.9
  229.2 1.3 dynamic-slice_bitcast_fusion.8
  230.5 1.4 fusion.305
  235.5 1.3 fusion.308
  236.8 1.3 dynamic-slice_bitcast_fusion.9
  238.1 1.3 dynamic-slice_bitcast_fusion.8
  239.3 1.4 fusion.305
  244.3 1.3 fusion.308
  245.6 1.3 dynamic-slice_bitcast_fusion.9
  246.9 1.3 dynamic-slice_bitcast_fusion.8
  248.2 1.4 fusion.305
  253.1 1.3 fusion.308
  254.4 1.3 dynamic-slice_bitcast_fusion.9
  255.7 1.3 dynamic-slice_bitcast_fusion.8
  257.0 1.4 fusion.305
  261.9 1.3 fusion.308
  263.2 1.3 dynamic-slice_bitcast_fusion.9
  264.5 1.3 dynamic-slice_bitcast_fusion.8
  265.8 1.4 fusion.305
  270.8 1.3 fusion.308
  272.1 1.3 dynamic-slice_bitcast_fusion.9
  273.4 1.3 dynamic-slice_bitcast_fusion.8
  274.6 1.4 fusion.305
  279.6 1.3 fusion.308
  280.9 1.3 dynamic-slice_bitcast_fusion.9
  282.2 1.3 dynamic-slice_bitcast_fusion.8
  283.5 1.4 fusion.305
  288.4 1.3 fusion.308
  289.7 1.3 dynamic-slice_bitcast_fusion.9
  291.0 1.3 dynamic-slice_bitcast_fusion.8
  292.3 1.4 fusion.305
  297.2 1.3 fusion.308
  298.5 1.3 copy.58
  300.0 1.7 pad_maximum_fusion.7
  301.6 7.6 %all-to-all-start = ((bf16[4,8,69,2,256]{4,1,3,2,0:T(8,128)(2,1)}), bf16[4,8,69,2,256]{4,1,3,2,0:T(8,128)(2,1)}, u32[]{:S(2)}, u32[]{:S(2)}) async-start(bf16[4,8,69,2,256]{4,1,3,2,0:T(8,128)(2,1)} %pad_maximum_fusion.7), calls=%async_computation | async-start | bytes 4521984 | tf_op jit(solution)/shard_map/all_to_all | solution.py:89
  309.3 26.6 %all-to-all-done = bf16[4,8,69,2,256]{4,1,3,2,0:T(8,128)(2,1)} async-done(((bf16[4,8,69,2,256]{4,1,3,2,0:T(8,128)(2,1)}), bf16[4,8,69,2,256]{4,1,3,2,0:T(8,128)(2,1)}, u32[]{:S(2)}, u32[]{:S(2)}) %all-to-all-start) | async-done | bytes 2261024 | tf_op jit(solution)/shard_map/all_to_all | solution.py:89
  336.0 2.4 copy.62
  339.9 9.3 %all-gather.5 = f32[4,2,1056]{2,1,0:T(2,128)S(1)} all-gather(f32[1,2,1056]{2,1,0:T(2,128)S(1)} %maximum_bitcast_fusion), channel_id=2, replica_groups=mesh['y_lo'=2,'core'=2,'y_hi'=2,'x'=4,'z'=4] {'z'}, dimensions={0}, use_global_device_ids=true | all-gather | bytes 42240 | tf_op jit(solution)/shard_map/all_gather | solution.py:117
  349.2 17.7 %all-gather.1 = f32[16,2,1056]{2,1,0:T(2,128)S(1)} all-gather(f32[4,2,1056]{2,1,0:T(2,128)S(1)} %all-gather.5), channel_id=3, replica_groups=mesh['y_lo'=2,'core'=2,'y_hi'=2,'x'=4,'z'=4] {'x'}, dimensions={0}, use_global_device_ids=true | all-gather | bytes 168960 | tf_op jit(solution)/shard_map/all_gather | solution.py:117
  366.9 6.2 %all-gather.2 = f32[8,4,2,1056]{3,1,2,0:T(4,128)S(1)} all-gather(f32[4,4,2,1056]{3,1,2,0:T(4,128)S(1)} %copy.63), channel_id=4, replica_groups=mesh['y_lo'=2,'core'=2,'y_hi'=2,'x'=4,'z'=4] {'y_hi'}, dimensions={0}, use_global_device_ids=true | all-gather | bytes 405504 | tf_op jit(solution)/shard_map/all_gather | solution.py:117
  373.1 9.4 %all-gather.3 = f32[4,4,4,2,1056]{4,2,3,1,0:T(4,128)} all-gather(f32[2,4,4,2,1056]{4,2,3,1,0:T(4,128)S(1)} %bitcast.289), channel_id=5, replica_groups=mesh['y_lo'=2,'core'=2,'y_hi'=2,'x'=4,'z'=4] {'core'}, dimensions={0}, use_global_device_ids=true | all-gather | bytes 811008 | tf_op jit(solution)/shard_map/all_gather | solution.py:117
  382.6 2.5 convert_bitcast_fusion
  385.1 5.1 %reshape.59 = f32[2,32,17664]{2,1,0:T(8,128)} reshape(f32[2,32,69,256]{3,2,1,0:T(8,128)} %convert_bitcast_fusion) | data formatting | bytes 9043968 | tf_op jit(solution)/shard_map/convert_element_type | solution.py:151
  390.7 15.9 %all-gather.8.cloned.1.call-done = f32[4,2,4,4,2,1056]{5,3,4,2,1,0:T(4,128)} async-done(((f32[2,2,4,4,2,1056]{5,3,4,2,1,0:T(4,128)}), f32[4,2,4,4,2,1056]{5,3,4,2,1,0:T(4,128)}) %all-gather.8.cloned.1.call-update) | async-done | bytes 1081360 | tf_op jit(solution)/shard_map/all_gather | solution.py:117
  406.6 1.9 copy.64
  413.6 7.4 %convolution_add_fusion.7 = f32[2,32,17664]{2,1,0:T(8,128)} fusion(f32[2,32,17664]{2,1,0:T(8,128)} %reshape.59, f32[2,17664]{1,0:T(2,128)S(1)} %bitcast.291, f32[2,32,32]{2,1,0:T(8,128)S(1)} %fusion.164, f32[2,32]{1,0:T(2,128)S(1)} %broadcast_divide_fusion.3, f32[2]{0:T(128)S(1)} %get-tuple-element.176), kind=kOutput, calls=%fused_computation.144 | convolution fusion | flops 436375552 | bytes 9193736 | tf_op jit(solution)/shard_map/pkm,pkc->pmc/dot_general | solution.py:154
  421.0 5.1 %reshape.57 = f32[2,32,69,256]{3,2,1,0:T(8,128)} reshape(f32[2,32,17664]{2,1,0:T(8,128)} %convolution_add_fusion.7) | data formatting | bytes 9043968 | tf_op jit(solution)/shard_map/reshape | solution.py:157
  426.1 7.9 %copy.66 = f32[32,69,2,256]{3,2,1,0:T(2,128)} copy(f32[32,69,2,256]{3,1,0,2:T(8,128)} %bitcast.287) | data formatting | bytes 9043968 | tf_op jit(solution)/shard_map/transpose | solution.py:157
  (256 shorter events, 109.4 us)
Async XLA Ops:
  12.9 8.3 %copy-start = (bf16[8,69,2,1024]{3,2,1,0:T(2,128)(2,1)S(1)}, bf16[8,69,2,1024]{3,2,1,0:T(2,128)(2,1)}, u32[]{:S(2)}) copy-start(bf16[8,69,2,1024]{3,2,1,0:T(2,128)(2,1)} %param.14) | copy-start | bytes 6782980
  12.9 28.1 %collective-permute-start = (bf16[8,69,1,1024]{3,0,2,1:T(8,128)(2,1)S(1)}, bf16[8,69,1,1024]{3,0,2,1:T(8,128)(2,1)}, u32[]{:S(2)}, u32[]{:S(2)}) collective-permute-start(bf16[8,69,1,1024]{3,0,2,1:T(8,128)(2,1)S(1)} %copy.77), channel_id=1, source_target_pairs={{0,1},{1,2},{2,3},{3,4},{4,5},{5,6},{6,7},{7,8},{8,9},{9,10},{10,1... | collective-permute-start | bytes 3391496 | tf_op jit(solution)/shard_map/ppermute | solution.py:23
  19.8 27.7 %collective-permute-start.1 = (bf16[8,69,1,1024]{3,0,2,1:T(8,128)(2,1)}, bf16[8,69,1,1024]{3,0,2,1:T(8,128)(2,1)}, u32[]{:S(2)}, u32[]{:S(2)}) collective-permute-start(bf16[8,69,1,1024]{3,0,2,1:T(8,128)(2,1)} %copy.78), channel_id=1, source_target_pairs={{1,0},{2,1},{3,2},{4,3},{5,4},{6,5},{7,6},{8,7},{9,8},{10,9},{11,1... | collective-permute-start | bytes 3391496 | tf_op jit(solution)/shard_map/ppermute | solution.py:25
  21.9 27.5 %copy-start.1 = (bf16[8,69,2,1024]{3,1,2,0:T(8,128)(2,1)}, bf16[8,69,2,1024]{3,1,2,0:T(8,128)(2,1)S(1)}, u32[]{:S(2)}) copy-start(bf16[8,69,2,1024]{3,1,2,0:T(8,128)(2,1)S(1)} %copy.56) | copy-start | bytes 6782980
  49.4 2.5 copy-start.2
  49.4 2.5 copy-start.4
  125.3 102.7 %copy-start.3 = (bf16[3,3,69,256]{3,2,1,0:T(8,128)(2,1)S(1)}, bf16[3,3,69,256]{3,2,1,0:T(8,128)(2,1)}, u32[]{:S(2)}) copy-start(bf16[3,3,69,256]{3,2,1,0:T(8,128)(2,1)} %param.17) | copy-start | bytes 953860
  125.3 102.7 %copy-start.10 = (f32[69]{0:T(128)S(1)}, f32[69]{0:T(128)}, u32[]{:S(2)}) copy-start(f32[69]{0:T(128)} %param.18) | copy-start | bytes 832
  131.3 90.8 %collective-permute-start.2 = (bf16[8,256,1,1024]{3,1,2,0:T(8,128)(2,1)}, bf16[8,256,1,1024]{3,1,2,0:T(8,128)(2,1)}, u32[]{:S(2)}, u32[]{:S(2)}) collective-permute-start(bf16[8,256,1,1024]{3,1,2,0:T(8,128)(2,1)} %get-tuple-element.165), channel_id=1, source_target_pairs={{0,1},{1,2},{2,3},{3,4},{4,5},{5,6},{6,7},{7,8},{8,9},{9,10},{10,1... | collective-permute-start | bytes 12582920 | tf_op jit(solution)/shard_map/ppermute | solution.py:70
  135.8 92.1 %collective-permute-start.3 = (bf16[8,256,1,1024]{3,1,2,0:T(8,128)(2,1)}, bf16[8,256,1,1024]{3,1,2,0:T(8,128)(2,1)}, u32[]{:S(2)}, u32[]{:S(2)}) collective-permute-start(bf16[8,256,1,1024]{3,1,2,0:T(8,128)(2,1)} %get-tuple-element.164), channel_id=1, source_target_pairs={{1,0},{2,1},{3,2},{4,3},{5,4},{6,5},{7,6},{8,7},{9,8},{10,9},{11,1... | collective-permute-start | bytes 12582920 | tf_op jit(solution)/shard_map/ppermute | solution.py:73
  301.6 7.7 %copy-start.6 = (s32[2,256]{1,0:T(2,128)S(1)}, s32[2,256]{1,0:T(2,128)}, u32[]{:S(2)}) copy-start(s32[2,256]{1,0:T(2,128)} %param.19) | copy-start | bytes 6148
  301.6 34.3 %all-to-all-start = ((bf16[4,8,69,2,256]{4,1,3,2,0:T(8,128)(2,1)}), bf16[4,8,69,2,256]{4,1,3,2,0:T(8,128)(2,1)}, u32[]{:S(2)}, u32[]{:S(2)}) async-start(bf16[4,8,69,2,256]{4,1,3,2,0:T(8,128)(2,1)} %pad_maximum_fusion.7), calls=%async_computation | async-start | bytes 4521984 | tf_op jit(solution)/shard_map/all_to_all | solution.py:89
  309.3 97.3 %all-gather.8.cloned.1.call-start = ((), (), s32[]{:S(2)}) async-start(), calls=%async_computation.1 | async-start | bytes 1769472 | tf_op jit(solution)/shard_map/all_gather | solution.py:117
  338.4 1.0 copy-start.5
  338.4 1.0 copy-start.7
  339.3 43.2 %copy-start.8 = (f32[2,8]{1,0:T(2,128)S(1)}, f32[2,8]{1,0:T(2,128)}, u32[]{:S(2)}) copy-start(f32[2,8]{1,0:T(2,128)} %param.23) | copy-start | bytes 196
  339.3 43.1 %copy-start.9 = (s32[2,8]{1,0:T(2,128)S(1)}, s32[2,8]{1,0:T(2,128)}, u32[]{:S(2)}) copy-start(s32[2,8]{1,0:T(2,128)} %param.22) | copy-start | bytes 196
Sparse Core Ops, SparseCore 0:
  382.6 23.9 all-gather.7
